TPU v7x, 32 devices: a whole 2x2x4 slice. The times are simulated.
32 devices in a mesh: section: 2 (over core), row: 4 (over y, x), col: 4 (over z).
Axes of the slice: x: 2, y: 2, z: 4, core: 2. Of those that a mesh axis runs over, the one named last changes fastest.
Arguments:
- checkpoints: bfloat16 [2, 4, 64, 128, 128], P('section', None, 'row', 'col'), may hold values from -1 to 1
- kernels: bfloat16 [4, 3, 3, 128, 128], P('section'), may hold values from -0.25 to 0.25
- cotangent: bfloat16 [4, 64, 128, 128], P(None, 'row', 'col'), may hold values from -1.5 to 1.5
- plan: int32 [4], replicated, may hold values from 0 to 3, each once
Outputs:
- boundary_grad: bfloat16 [2, 4, 64, 128, 128], P('section', None, 'row', 'col')
- kernel_grad: float32 [4, 3, 3, 128, 128], P('section')
Inputs may be any that keep to these rules, and one draw needn't show every extreme that they name: plan names each of the 4 microbatches exactly once; slot k of cotangent belongs to microbatch plan[k].
All inputs are finite; a program needn't handle non-finite values.
Results may differ from a plain program's by a relative error of at most 0.015.
Values may be sent and summed in bfloat16 or wider, within the bound.
No kernel may reach another device: no remote copies, remote signals or barrier semaphores. Data moves between devices by JAX's collectives and lax.ppermute only.
A program may use at most 64 MiB of HBM per device.

v0:
```python
import jax
import jax.numpy as jnp
from jax import lax
from jax.sharding import PartitionSpec as P


def extended(block, sides, width):
    for axis, dim in sides:
        count = lax.axis_size(axis)
        forward = [(i, i + 1) for i in range(count - 1)]
        backward = [(target, source) for source, target in forward]
        low = lax.ppermute(
            lax.slice_in_dim(block, block.shape[dim] - width, None, axis=dim), axis, forward
        )
        high = lax.ppermute(lax.slice_in_dim(block, 0, width, axis=dim), axis, backward)
        block = jnp.concatenate([low, block, high], axis=dim)
    return block


def passed_along(block, axis, distance):
    devices = range(lax.axis_size(axis))
    route = [(i - distance, i) for i in devices if i - distance in devices]
    return lax.ppermute(block, axis, route)


def convolve(padded, kernel):
    return lax.conv_general_dilated(
        padded,
        kernel,
        (1, 1),
        "VALID",
        dimension_numbers=("NHWC", "HWIO", "NHWC"),
        preferred_element_type=jnp.float32,
    )


def take_slots(values_in, slot_first, group_size):
    return lax.dynamic_slice_in_dim(values_in, slot_first, group_size, 0)


def kernel_terms(padded, signal):
    channels = signal.shape[3]
    flat_signal = signal.reshape(-1, channels)
    rows_out = []
    for a in range(3):
        tap_row = []
        for b in range(3):
            window = padded[:, a : a + signal.shape[1], b : b + signal.shape[2]].reshape(
                -1, channels
            )
            tap_row.append(
                lax.dot_general(
                    window,
                    flat_signal,
                    (((0,), (0,)), ((), ())),
                    preferred_element_type=jnp.float32,
                )
            )
        rows_out.append(jnp.stack(tap_row))
    return jnp.stack(rows_out)


def local(checkpoints, kernels, cotangent, plan):
    sections_count = lax.axis_size("section")
    section_index = lax.axis_index("section")
    batches = checkpoints.shape[1]
    tile_rows = checkpoints.shape[2]
    tile_cols = checkpoints.shape[3]
    channels = checkpoints.shape[4]
    layer_count = kernels.shape[0]
    flipped = jnp.transpose(kernels[:, ::-1, ::-1], (0, 1, 2, 4, 3))
    first_input = jnp.take(checkpoints[0], plan, axis=0)
    inputs_list = []
    outputs_list = []
    input_margin = []
    output_margin = []
    current = first_input
    for layer_idx in range(layer_count):
        padded = extended(current, (("row", 1), ("col", 2)), 1)
        inputs_list.append(padded)
        input_margin.append(1)
        current = jnp.tanh(convolve(padded, kernels[layer_idx])).astype(jnp.bfloat16)
        outputs_list.append(current)
        output_margin.append(0)
    groups = batches // batches
    tick_count = groups + sections_count - 1

    def backward(top_grad, slot_first):
        signals = [None] * layer_count
        gradient = top_grad.astype(jnp.float32)
        for layer_idx in reversed(range(layer_count)):
            output = take_slots(outputs_list[layer_idx], slot_first, batches).astype(jnp.float32)
            signal = (gradient * (1.0 - output * output)).astype(jnp.bfloat16)
            signals[layer_idx] = signal
            padded = extended(signal, (("row", 1), ("col", 2)), 1)
            gradient = convolve(padded, flipped[layer_idx])
        return (gradient.astype(jnp.bfloat16), signals)

    def tick_step(tick_idx, loop_state):
        incoming, boundary, gathered = loop_state
        slot_group = tick_idx - (sections_count - 1 - section_index)
        is_valid = (slot_group >= 0) & (slot_group < groups)
        slot_first = jnp.clip(slot_group, 0, groups - 1) * batches
        top_grad = jnp.where(section_index == sections_count - 1, cotangent, incoming)
        result, signals = backward(top_grad, slot_first)
        previous = boundary
        boundary = lax.dynamic_update_slice_in_dim(
            boundary, jnp.where(is_valid, result, previous), slot_first, 0
        )
        tap_terms = jnp.stack(
            [
                kernel_terms(
                    take_slots(inputs_list[layer_idx], slot_first, batches), signals[layer_idx]
                )
                for layer_idx in range(layer_count)
            ]
        )
        gathered = gathered + jnp.where(is_valid, tap_terms, 0.0)
        incoming = passed_along(result, "section", -1)
        return (incoming, boundary, gathered)

    incoming_zero = jnp.zeros((batches, tile_rows, tile_cols, channels), jnp.bfloat16)
    boundary_zero = jnp.zeros((batches, tile_rows, tile_cols, channels), jnp.bfloat16)
    gathered_zero = jnp.zeros((layer_count, 3, 3, channels, channels), jnp.float32)
    incoming, boundary, gathered = lax.fori_loop(
        0, tick_count, tick_step, (incoming_zero, boundary_zero, gathered_zero)
    )
    kernel_grad = (
        lax.psum(gathered.astype(jnp.bfloat16), ("row", "col")).astype(jnp.float32) / batches
    )
    boundary_grad = jnp.zeros_like(boundary).at[plan].set(boundary)[None]
    return (boundary_grad, kernel_grad)


def solution(mesh):
    return jax.shard_map(
        local,
        mesh=mesh,
        in_specs=(
            P("section", None, "row", "col", None),
            P("section", None, None, None, None),
            P(None, "row", "col", None),
            P(),
        ),
        out_specs=(P("section", None, "row", "col", None), P("section", None, None, None, None)),
        check_vma=False,
    )
```

profile of v0, /device:TPU:0, one launch (start us, length us, event | category | flops | bytes accessed | tf_op | source)
XLA Modules:
  0.0 291.0 jit_solution(17927654028252971086)
XLA Ops:
  10.8 5.5 %collective-permute-start.9 = (bf16[4,1,32,128]{3,2,1,0:T(8,128)(2,1)S(1)}, bf16[4,1,32,128]{3,2,1,0:T(8,128)(2,1)S(1)}, u32[]{:S(2)}, u32[]{:S(2)}) collective-permute-start(bf16[4,1,32,128]{3,2,1,0:T(8,128)(2,1)S(1)} %get-tuple-element.383), channel_id=1, source_target_pairs={{0,4},{4,8},{8,12},{1,5},{5,9},{9,13},{2,6},{6,10},{10,14},{3,7},{... | collective-permute-start | bytes 98312 | tf_op jit(solution)/shard_map/ppermute | solution.py:12
  18.5 4.0 %collective-permute-start.11 = (bf16[4,18,1,128]{3,2,1,0:T(2,128)(2,1)}, bf16[4,18,1,128]{3,2,1,0:T(2,128)(2,1)S(1)}, u32[]{:S(2)}, u32[]{:S(2)}) collective-permute-start(bf16[4,18,1,128]{3,2,1,0:T(2,128)(2,1)} %get-tuple-element.381), channel_id=1, source_target_pairs={{0,1},{1,2},{2,3},{4,5},{5,6},{6,7},{8,9},{9,10},{10,11},{12,13},{... | collective-permute-start | bytes 55304 | tf_op jit(solution)/shard_map/ppermute | solution.py:12
  26.0 2.6 collective-permute-done.12
  30.2 1.7 fusion.39
  35.1 4.9 %collective-permute-start.13 = (bf16[4,1,32,128]{3,2,0,1:T(8,128)(2,1)S(1)}, bf16[4,1,32,128]{3,2,0,1:T(8,128)(2,1)S(1)}, u32[]{:S(2)}, u32[]{:S(2)}) collective-permute-start(bf16[4,1,32,128]{3,2,0,1:T(8,128)(2,1)S(1)} %slice_bitcast_fusion.5), channel_id=1, source_target_pairs={{0,4},{4,8},{8,12},{1,5},{5,9},{9,13},{2,6},{6,10},{10,14},{3,7},{... | collective-permute-start | bytes 98312 | tf_op jit(solution)/shard_map/ppermute | solution.py:12
  41.7 3.5 %collective-permute-start.15 = (bf16[4,18,1,128]{3,1,2,0:T(8,128)(2,1)S(1)}, bf16[4,18,1,128]{3,1,2,0:T(8,128)(2,1)S(1)}, u32[]{:S(2)}, u32[]{:S(2)}) collective-permute-start(bf16[4,18,1,128]{3,1,2,0:T(8,128)(2,1)S(1)} %get-tuple-element.377), channel_id=1, source_target_pairs={{0,1},{1,2},{2,3},{4,5},{5,6},{6,7},{8,9},{9,10},{10,11},{12,13},{... | collective-permute-start | bytes 55304 | tf_op jit(solution)/shard_map/ppermute | solution.py:12
  48.0 3.0 %collective-permute-done.16 = bf16[4,18,1,128]{3,1,2,0:T(8,128)(2,1)S(1)} collective-permute-done((bf16[4,18,1,128]{3,1,2,0:T(8,128)(2,1)S(1)}, bf16[4,18,1,128]{3,1,2,0:T(8,128)(2,1)S(1)}, u32[]{:S(2)}, u32[]{:S(2)}) %collective-permute-start.16) | collective-permute-done | bytes 18464 | tf_op jit(solution)/shard_map/ppermute | solution.py:15
  50.9 1.4 pad_maximum_fusion.6
  53.9 1.7 fusion.38
  57.6 106.7 %while.20 = (s32[]{:T(128)}, bf16[4,16,32,128]{3,1,2,0:T(8,128)(2,1)}, bf16[4,16,32,128]{3,1,2,0:T(8,128)(2,1)}, f32[2,3,3,128,128]{3,4,2,1,0:T(8,128)S(1)}, pre...) while((s32[]{:T(128)}, ...), condition=%wide.region_1.2_spmd.clone, body=%wide.region_0.1_spmd.clone.sunk | while | flops 2737602560 | bytes 72510144 | solution.py:125
  57.6 1.7 multiply_convert_fusion.2
  60.7 5.8 %collective-permute-start.1 = (bf16[4,1,32,128]{3,1,2,0:T(2,128)(2,1)S(1)}, bf16[4,1,32,128]{3,1,2,0:T(2,128)(2,1)S(1)}, u32[]{:S(2)}, u32[]{:S(2)}) collective-permute-start(bf16[4,1,32,128]{3,1,2,0:T(2,128)(2,1)S(1)} %get-tuple-element.471), channel_id=1, source_target_pairs={{0,4},{4,8},{8,12},{1,5},{5,9},{9,13},{2,6},{6,10},{10,14},{3,7},{... | collective-permute-start | bytes 98312 | tf_op jit(solution)/shard_map/while/body/eval_jaxpr/ppermute | solution.py:12
  71.0 5.2 %collective-permute-start.3 = (bf16[4,18,1,128]{3,1,2,0:T(8,128)(2,1)S(1)}, bf16[4,18,1,128]{3,1,2,0:T(8,128)(2,1)}, u32[]{:S(2)}, u32[]{:S(2)}) collective-permute-start(bf16[4,18,1,128]{3,1,2,0:T(8,128)(2,1)S(1)} %get-tuple-element.473), channel_id=1, source_target_pairs={{0,1},{1,2},{2,3},{4,5},{5,6},{6,7},{8,9},{9,10},{10,11},{12,13},{... | collective-permute-start | bytes 55304 | tf_op jit(solution)/shard_map/while/body/eval_jaxpr/ppermute | solution.py:12
  79.8 1.7 convolution_select_fusion.5
  88.0 5.7 %collective-permute-start.5 = (bf16[4,1,32,128]{3,1,2,0:T(2,128)(2,1)S(1)}, bf16[4,1,32,128]{3,1,2,0:T(2,128)(2,1)S(1)}, u32[]{:S(2)}, u32[]{:S(2)}) collective-permute-start(bf16[4,1,32,128]{3,1,2,0:T(2,128)(2,1)S(1)} %get-tuple-element.475), channel_id=1, source_target_pairs={{0,4},{4,8},{8,12},{1,5},{5,9},{9,13},{2,6},{6,10},{10,14},{3,7},{... | collective-permute-start | bytes 98312 | tf_op jit(solution)/shard_map/while/body/eval_jaxpr/ppermute | solution.py:12
  94.0 1.6 collective-permute-done.5
  96.9 4.9 %collective-permute-start.7 = (bf16[4,18,1,128]{3,1,2,0:T(8,128)(2,1)S(1)}, bf16[4,18,1,128]{3,1,2,0:T(8,128)(2,1)S(1)}, u32[]{:S(2)}, u32[]{:S(2)}) collective-permute-start(bf16[4,18,1,128]{3,1,2,0:T(8,128)(2,1)S(1)} %get-tuple-element.477), channel_id=1, source_target_pairs={{0,1},{1,2},{2,3},{4,5},{5,6},{6,7},{8,9},{9,10},{10,11},{12,13},{... | collective-permute-start | bytes 55304 | tf_op jit(solution)/shard_map/while/body/eval_jaxpr/ppermute | solution.py:12
  102.0 1.4 collective-permute-done.7
  104.9 1.7 fusion.166
  109.5 1.3 collective-permute-done.8
  110.9 1.7 multiply_convert_fusion.2
  114.0 5.4 %collective-permute-start.1 = (bf16[4,1,32,128]{3,1,2,0:T(2,128)(2,1)S(1)}, bf16[4,1,32,128]{3,1,2,0:T(2,128)(2,1)S(1)}, u32[]{:S(2)}, u32[]{:S(2)}) collective-permute-start(bf16[4,1,32,128]{3,1,2,0:T(2,128)(2,1)S(1)} %get-tuple-element.471), channel_id=1, source_target_pairs={{0,4},{4,8},{8,12},{1,5},{5,9},{9,13},{2,6},{6,10},{10,14},{3,7},{... | collective-permute-start | bytes 98312 | tf_op jit(solution)/shard_map/while/body/eval_jaxpr/ppermute | solution.py:12
  124.0 5.5 %collective-permute-start.3 = (bf16[4,18,1,128]{3,1,2,0:T(8,128)(2,1)S(1)}, bf16[4,18,1,128]{3,1,2,0:T(8,128)(2,1)}, u32[]{:S(2)}, u32[]{:S(2)}) collective-permute-start(bf16[4,18,1,128]{3,1,2,0:T(8,128)(2,1)S(1)} %get-tuple-element.473), channel_id=1, source_target_pairs={{0,1},{1,2},{2,3},{4,5},{5,6},{6,7},{8,9},{9,10},{10,11},{12,13},{... | collective-permute-start | bytes 55304 | tf_op jit(solution)/shard_map/while/body/eval_jaxpr/ppermute | solution.py:12
  133.1 1.7 convolution_select_fusion.5
  141.3 5.8 %collective-permute-start.5 = (bf16[4,1,32,128]{3,1,2,0:T(2,128)(2,1)S(1)}, bf16[4,1,32,128]{3,1,2,0:T(2,128)(2,1)S(1)}, u32[]{:S(2)}, u32[]{:S(2)}) collective-permute-start(bf16[4,1,32,128]{3,1,2,0:T(2,128)(2,1)S(1)} %get-tuple-element.475), channel_id=1, source_target_pairs={{0,4},{4,8},{8,12},{1,5},{5,9},{9,13},{2,6},{6,10},{10,14},{3,7},{... | collective-permute-start | bytes 98312 | tf_op jit(solution)/shard_map/while/body/eval_jaxpr/ppermute | solution.py:12
  147.4 1.6 collective-permute-done.5
  150.3 4.9 %collective-permute-start.7 = (bf16[4,18,1,128]{3,1,2,0:T(8,128)(2,1)S(1)}, bf16[4,18,1,128]{3,1,2,0:T(8,128)(2,1)S(1)}, u32[]{:S(2)}, u32[]{:S(2)}) collective-permute-start(bf16[4,18,1,128]{3,1,2,0:T(8,128)(2,1)S(1)} %get-tuple-element.477), channel_id=1, source_target_pairs={{0,1},{1,2},{2,3},{4,5},{5,6},{6,7},{8,9},{9,10},{10,11},{12,13},{... | collective-permute-start | bytes 55304 | tf_op jit(solution)/shard_map/while/body/eval_jaxpr/ppermute | solution.py:12
  155.3 1.4 collective-permute-done.7
  158.3 1.7 fusion.166
  162.0 2.0 select_select_fusion.2
  167.4 114.6 %all-reduce.2.cloned.1.call-done = bf16[2,3,3,128,128]{4,3,2,1,0:T(8,128)(2,1)} async-done(((bf16[2,3,3,128,128]{4,3,2,1,0:T(8,128)(2,1)}), bf16[2,3,3,128,128]{4,3,2,1,0:T(8,128)(2,1)}) %all-reduce.2.cloned.1.call-update) | async-done | bytes 589840 | tf_op jit(solution)/shard_map/psum | solution.py:129
  282.0 2.2 convert_multiply_fusion
  (198 shorter events, 68.0 us)
Async XLA Ops:
  7.2 9.1 %copy-start.6 = (bf16[2,3,3,128,128]{4,3,2,1,0:T(8,128)(2,1)S(1)}, bf16[2,3,3,128,128]{4,3,2,1,0:T(8,128)(2,1)}, u32[]{:S(2)}) copy-start(bf16[2,3,3,128,128]{4,3,2,1,0:T(8,128)(2,1)} %param.7) | copy-start | bytes 1769476
  7.2 274.8 %all-reduce.2.cloned.1.call-start = ((), (), s32[]{:S(2)}) async-start(), calls=%async_computation | async-start | bytes 1179648 | tf_op jit(solution)/shard_map/psum | solution.py:129
  9.5 7.1 %collective-permute-start.10 = (bf16[4,1,32,128]{3,2,1,0:T(8,128)(2,1)S(1)}, bf16[4,1,32,128]{3,2,1,0:T(8,128)(2,1)S(1)}, u32[]{:S(2)}, u32[]{:S(2)}) collective-permute-start(bf16[4,1,32,128]{3,2,1,0:T(8,128)(2,1)S(1)} %get-tuple-element.384), channel_id=1, source_target_pairs={{4,0},{8,4},{12,8},{5,1},{9,5},{13,9},{6,2},{10,6},{14,10},{7,3},{... | collective-permute-start | bytes 98312 | tf_op jit(solution)/shard_map/ppermute | solution.py:15
  10.8 7.1 %collective-permute-start.9 = (bf16[4,1,32,128]{3,2,1,0:T(8,128)(2,1)S(1)}, bf16[4,1,32,128]{3,2,1,0:T(8,128)(2,1)S(1)}, u32[]{:S(2)}, u32[]{:S(2)}) collective-permute-start(bf16[4,1,32,128]{3,2,1,0:T(8,128)(2,1)S(1)} %get-tuple-element.383), channel_id=1, source_target_pairs={{0,4},{4,8},{8,12},{1,5},{5,9},{9,13},{2,6},{6,10},{10,14},{3,7},{... | collective-permute-start | bytes 98312 | tf_op jit(solution)/shard_map/ppermute | solution.py:12
  18.5 7.5 %collective-permute-start.11 = (bf16[4,18,1,128]{3,2,1,0:T(2,128)(2,1)}, bf16[4,18,1,128]{3,2,1,0:T(2,128)(2,1)S(1)}, u32[]{:S(2)}, u32[]{:S(2)}) collective-permute-start(bf16[4,18,1,128]{3,2,1,0:T(2,128)(2,1)} %get-tuple-element.381), channel_id=1, source_target_pairs={{0,1},{1,2},{2,3},{4,5},{5,6},{6,7},{8,9},{9,10},{10,11},{12,13},{... | collective-permute-start | bytes 55304 | tf_op jit(solution)/shard_map/ppermute | solution.py:12
  22.5 6.1 %collective-permute-start.12 = (bf16[4,18,1,128]{3,2,1,0:T(2,128)(2,1)}, bf16[4,18,1,128]{3,2,1,0:T(2,128)(2,1)S(1)}, u32[]{:S(2)}, u32[]{:S(2)}) collective-permute-start(bf16[4,18,1,128]{3,2,1,0:T(2,128)(2,1)} %get-tuple-element.382), channel_id=1, source_target_pairs={{1,0},{2,1},{3,2},{5,4},{6,5},{7,6},{9,8},{10,9},{11,10},{13,12},{... | collective-permute-start | bytes 55304 | tf_op jit(solution)/shard_map/ppermute | solution.py:15
  33.8 7.9 %collective-permute-start.14 = (bf16[4,1,32,128]{3,1,2,0:T(2,128)(2,1)}, bf16[4,1,32,128]{3,1,2,0:T(2,128)(2,1)S(1)}, u32[]{:S(2)}, u32[]{:S(2)}) collective-permute-start(bf16[4,1,32,128]{3,1,2,0:T(2,128)(2,1)} %copy.87), channel_id=1, source_target_pairs={{4,0},{8,4},{12,8},{5,1},{9,5},{13,9},{6,2},{10,6},{14,10},{7,3},{... | collective-permute-start | bytes 98312 | tf_op jit(solution)/shard_map/ppermute | solution.py:15
  35.1 6.5 %collective-permute-start.13 = (bf16[4,1,32,128]{3,2,0,1:T(8,128)(2,1)S(1)}, bf16[4,1,32,128]{3,2,0,1:T(8,128)(2,1)S(1)}, u32[]{:S(2)}, u32[]{:S(2)}) collective-permute-start(bf16[4,1,32,128]{3,2,0,1:T(8,128)(2,1)S(1)} %slice_bitcast_fusion.5), channel_id=1, source_target_pairs={{0,4},{4,8},{8,12},{1,5},{5,9},{9,13},{2,6},{6,10},{10,14},{3,7},{... | collective-permute-start | bytes 98312 | tf_op jit(solution)/shard_map/ppermute | solution.py:12
  41.7 6.2 %collective-permute-start.15 = (bf16[4,18,1,128]{3,1,2,0:T(8,128)(2,1)S(1)}, bf16[4,18,1,128]{3,1,2,0:T(8,128)(2,1)S(1)}, u32[]{:S(2)}, u32[]{:S(2)}) collective-permute-start(bf16[4,18,1,128]{3,1,2,0:T(8,128)(2,1)S(1)} %get-tuple-element.377), channel_id=1, source_target_pairs={{0,1},{1,2},{2,3},{4,5},{5,6},{6,7},{8,9},{9,10},{10,11},{12,13},{... | collective-permute-start | bytes 55304 | tf_op jit(solution)/shard_map/ppermute | solution.py:12
  45.2 5.7 %collective-permute-start.16 = (bf16[4,18,1,128]{3,1,2,0:T(8,128)(2,1)S(1)}, bf16[4,18,1,128]{3,1,2,0:T(8,128)(2,1)S(1)}, u32[]{:S(2)}, u32[]{:S(2)}) collective-permute-start(bf16[4,18,1,128]{3,1,2,0:T(8,128)(2,1)S(1)} %get-tuple-element.378), channel_id=1, source_target_pairs={{1,0},{2,1},{3,2},{5,4},{6,5},{7,6},{9,8},{10,9},{11,10},{13,12},{... | collective-permute-start | bytes 55304 | tf_op jit(solution)/shard_map/ppermute | solution.py:15
  57.6 9.2 %copy-start.1 = (bf16[4,16,32,128]{3,1,2,0:T(8,128)(2,1)}, bf16[4,16,32,128]{3,1,2,0:T(8,128)(2,1)S(1)}, u32[]{:S(2)}) copy-start(bf16[4,16,32,128]{3,1,2,0:T(8,128)(2,1)S(1)} %get-tuple-element.519) | copy-start | bytes 1572868 | tf_op jit(solution)/shard_map/while
  57.6 8.9 %copy-start.4 = (bf16[4,18,34,128]{3,1,2,0:T(8,128)(2,1)S(1)}, bf16[4,18,34,128]{3,1,2,0:T(8,128)(2,1)}, u32[]{:S(2)}) copy-start(bf16[4,18,34,128]{3,1,2,0:T(8,128)(2,1)} %get-tuple-element.525) | copy-start | bytes 1880068 | tf_op jit(solution)/shard_map/while
  59.4 10.2 %collective-permute-start = (bf16[4,1,32,128]{3,1,2,0:T(2,128)(2,1)S(1)}, bf16[4,1,32,128]{3,1,2,0:T(2,128)(2,1)S(1)}, u32[]{:S(2)}, u32[]{:S(2)}) collective-permute-start(bf16[4,1,32,128]{3,1,2,0:T(2,128)(2,1)S(1)} %get-tuple-element.470), channel_id=1, source_target_pairs={{4,0},{8,4},{12,8},{5,1},{9,5},{13,9},{6,2},{10,6},{14,10},{7,3},{... | collective-permute-start | bytes 98312 | tf_op jit(solution)/shard_map/while/body/eval_jaxpr/ppermute | solution.py:15
  60.7 8.9 %collective-permute-start.1 = (bf16[4,1,32,128]{3,1,2,0:T(2,128)(2,1)S(1)}, bf16[4,1,32,128]{3,1,2,0:T(2,128)(2,1)S(1)}, u32[]{:S(2)}, u32[]{:S(2)}) collective-permute-start(bf16[4,1,32,128]{3,1,2,0:T(2,128)(2,1)S(1)} %get-tuple-element.471), channel_id=1, source_target_pairs={{0,4},{4,8},{8,12},{1,5},{5,9},{9,13},{2,6},{6,10},{10,14},{3,7},{... | collective-permute-start | bytes 98312 | tf_op jit(solution)/shard_map/while/body/eval_jaxpr/ppermute | solution.py:12
  69.7 6.5 %collective-permute-start.2 = (bf16[4,18,1,128]{3,1,2,0:T(8,128)(2,1)S(1)}, bf16[4,18,1,128]{3,1,2,0:T(8,128)(2,1)S(1)}, u32[]{:S(2)}, u32[]{:S(2)}) collective-permute-start(bf16[4,18,1,128]{3,1,2,0:T(8,128)(2,1)S(1)} %get-tuple-element.472), channel_id=1, source_target_pairs={{1,0},{2,1},{3,2},{5,4},{6,5},{7,6},{9,8},{10,9},{11,10},{13,12},{... | collective-permute-start | bytes 55304 | tf_op jit(solution)/shard_map/while/body/eval_jaxpr/ppermute | solution.py:15
  71.0 6.1 %collective-permute-start.3 = (bf16[4,18,1,128]{3,1,2,0:T(8,128)(2,1)S(1)}, bf16[4,18,1,128]{3,1,2,0:T(8,128)(2,1)}, u32[]{:S(2)}, u32[]{:S(2)}) collective-permute-start(bf16[4,18,1,128]{3,1,2,0:T(8,128)(2,1)S(1)} %get-tuple-element.473), channel_id=1, source_target_pairs={{0,1},{1,2},{2,3},{4,5},{5,6},{6,7},{8,9},{9,10},{10,11},{12,13},{... | collective-permute-start | bytes 55304 | tf_op jit(solution)/shard_map/while/body/eval_jaxpr/ppermute | solution.py:12
  86.7 7.4 %collective-permute-start.4 = (bf16[4,1,32,128]{3,1,2,0:T(2,128)(2,1)S(1)}, bf16[4,1,32,128]{3,1,2,0:T(2,128)(2,1)S(1)}, u32[]{:S(2)}, u32[]{:S(2)}) collective-permute-start(bf16[4,1,32,128]{3,1,2,0:T(2,128)(2,1)S(1)} %get-tuple-element.474), channel_id=1, source_target_pairs={{4,0},{8,4},{12,8},{5,1},{9,5},{13,9},{6,2},{10,6},{14,10},{7,3},{... | collective-permute-start | bytes 98312 | tf_op jit(solution)/shard_map/while/body/eval_jaxpr/ppermute | solution.py:15
  88.0 7.6 %collective-permute-start.5 = (bf16[4,1,32,128]{3,1,2,0:T(2,128)(2,1)S(1)}, bf16[4,1,32,128]{3,1,2,0:T(2,128)(2,1)S(1)}, u32[]{:S(2)}, u32[]{:S(2)}) collective-permute-start(bf16[4,1,32,128]{3,1,2,0:T(2,128)(2,1)S(1)} %get-tuple-element.475), channel_id=1, source_target_pairs={{0,4},{4,8},{8,12},{1,5},{5,9},{9,13},{2,6},{6,10},{10,14},{3,7},{... | collective-permute-start | bytes 98312 | tf_op jit(solution)/shard_map/while/body/eval_jaxpr/ppermute | solution.py:12
  95.6 6.3 %collective-permute-start.6 = (bf16[4,18,1,128]{3,1,2,0:T(8,128)(2,1)S(1)}, bf16[4,18,1,128]{3,1,2,0:T(8,128)(2,1)S(1)}, u32[]{:S(2)}, u32[]{:S(2)}) collective-permute-start(bf16[4,18,1,128]{3,1,2,0:T(8,128)(2,1)S(1)} %get-tuple-element.476), channel_id=1, source_target_pairs={{1,0},{2,1},{3,2},{5,4},{6,5},{7,6},{9,8},{10,9},{11,10},{13,12},{... | collective-permute-start | bytes 55304 | tf_op jit(solution)/shard_map/while/body/eval_jaxpr/ppermute | solution.py:15
  96.9 6.5 %collective-permute-start.7 = (bf16[4,18,1,128]{3,1,2,0:T(8,128)(2,1)S(1)}, bf16[4,18,1,128]{3,1,2,0:T(8,128)(2,1)S(1)}, u32[]{:S(2)}, u32[]{:S(2)}) collective-permute-start(bf16[4,18,1,128]{3,1,2,0:T(8,128)(2,1)S(1)} %get-tuple-element.477), channel_id=1, source_target_pairs={{0,1},{1,2},{2,3},{4,5},{5,6},{6,7},{8,9},{9,10},{10,11},{12,13},{... | collective-permute-start | bytes 55304 | tf_op jit(solution)/shard_map/while/body/eval_jaxpr/ppermute | solution.py:12
  107.0 3.9 %collective-permute-start.8 = (bf16[4,16,32,128]{3,1,2,0:T(8,128)(2,1)S(1)}, bf16[4,16,32,128]{3,1,2,0:T(8,128)(2,1)}, u32[]{:S(2)}, u32[]{:S(2)}) collective-permute-start(bf16[4,16,32,128]{3,1,2,0:T(8,128)(2,1)S(1)} %slice_bitcast_fusion.7), channel_id=1, source_target_pairs={{16,0},{17,1},{18,2},{19,3},{20,4},{21,5},{22,6},{23,7},{24,8},{25... | collective-permute-start | bytes 1572872 | tf_op jit(solution)/shard_map/while/body/eval_jaxpr/ppermute | solution.py:23
  110.9 8.9 %copy-start.1 = (bf16[4,16,32,128]{3,1,2,0:T(8,128)(2,1)}, bf16[4,16,32,128]{3,1,2,0:T(8,128)(2,1)S(1)}, u32[]{:S(2)}) copy-start(bf16[4,16,32,128]{3,1,2,0:T(8,128)(2,1)S(1)} %get-tuple-element.519) | copy-start | bytes 1572868 | tf_op jit(solution)/shard_map/while
  112.7 9.9 %collective-permute-start = (bf16[4,1,32,128]{3,1,2,0:T(2,128)(2,1)S(1)}, bf16[4,1,32,128]{3,1,2,0:T(2,128)(2,1)S(1)}, u32[]{:S(2)}, u32[]{:S(2)}) collective-permute-start(bf16[4,1,32,128]{3,1,2,0:T(2,128)(2,1)S(1)} %get-tuple-element.470), channel_id=1, source_target_pairs={{4,0},{8,4},{12,8},{5,1},{9,5},{13,9},{6,2},{10,6},{14,10},{7,3},{... | collective-permute-start | bytes 98312 | tf_op jit(solution)/shard_map/while/body/eval_jaxpr/ppermute | solution.py:15
  114.0 8.6 %collective-permute-start.1 = (bf16[4,1,32,128]{3,1,2,0:T(2,128)(2,1)S(1)}, bf16[4,1,32,128]{3,1,2,0:T(2,128)(2,1)S(1)}, u32[]{:S(2)}, u32[]{:S(2)}) collective-permute-start(bf16[4,1,32,128]{3,1,2,0:T(2,128)(2,1)S(1)} %get-tuple-element.471), channel_id=1, source_target_pairs={{0,4},{4,8},{8,12},{1,5},{5,9},{9,13},{2,6},{6,10},{10,14},{3,7},{... | collective-permute-start | bytes 98312 | tf_op jit(solution)/shard_map/while/body/eval_jaxpr/ppermute | solution.py:12
  122.7 6.8 %collective-permute-start.2 = (bf16[4,18,1,128]{3,1,2,0:T(8,128)(2,1)S(1)}, bf16[4,18,1,128]{3,1,2,0:T(8,128)(2,1)S(1)}, u32[]{:S(2)}, u32[]{:S(2)}) collective-permute-start(bf16[4,18,1,128]{3,1,2,0:T(8,128)(2,1)S(1)} %get-tuple-element.472), channel_id=1, source_target_pairs={{1,0},{2,1},{3,2},{5,4},{6,5},{7,6},{9,8},{10,9},{11,10},{13,12},{... | collective-permute-start | bytes 55304 | tf_op jit(solution)/shard_map/while/body/eval_jaxpr/ppermute | solution.py:15
  124.0 6.4 %collective-permute-start.3 = (bf16[4,18,1,128]{3,1,2,0:T(8,128)(2,1)S(1)}, bf16[4,18,1,128]{3,1,2,0:T(8,128)(2,1)}, u32[]{:S(2)}, u32[]{:S(2)}) collective-permute-start(bf16[4,18,1,128]{3,1,2,0:T(8,128)(2,1)S(1)} %get-tuple-element.473), channel_id=1, source_target_pairs={{0,1},{1,2},{2,3},{4,5},{5,6},{6,7},{8,9},{9,10},{10,11},{12,13},{... | collective-permute-start | bytes 55304 | tf_op jit(solution)/shard_map/while/body/eval_jaxpr/ppermute | solution.py:12
  140.0 7.4 %collective-permute-start.4 = (bf16[4,1,32,128]{3,1,2,0:T(2,128)(2,1)S(1)}, bf16[4,1,32,128]{3,1,2,0:T(2,128)(2,1)S(1)}, u32[]{:S(2)}, u32[]{:S(2)}) collective-permute-start(bf16[4,1,32,128]{3,1,2,0:T(2,128)(2,1)S(1)} %get-tuple-element.474), channel_id=1, source_target_pairs={{4,0},{8,4},{12,8},{5,1},{9,5},{13,9},{6,2},{10,6},{14,10},{7,3},{... | collective-permute-start | bytes 98312 | tf_op jit(solution)/shard_map/while/body/eval_jaxpr/ppermute | solution.py:15
  141.3 7.7 %collective-permute-start.5 = (bf16[4,1,32,128]{3,1,2,0:T(2,128)(2,1)S(1)}, bf16[4,1,32,128]{3,1,2,0:T(2,128)(2,1)S(1)}, u32[]{:S(2)}, u32[]{:S(2)}) collective-permute-start(bf16[4,1,32,128]{3,1,2,0:T(2,128)(2,1)S(1)} %get-tuple-element.475), channel_id=1, source_target_pairs={{0,4},{4,8},{8,12},{1,5},{5,9},{9,13},{2,6},{6,10},{10,14},{3,7},{... | collective-permute-start | bytes 98312 | tf_op jit(solution)/shard_map/while/body/eval_jaxpr/ppermute | solution.py:12
  149.0 6.3 %collective-permute-start.6 = (bf16[4,18,1,128]{3,1,2,0:T(8,128)(2,1)S(1)}, bf16[4,18,1,128]{3,1,2,0:T(8,128)(2,1)S(1)}, u32[]{:S(2)}, u32[]{:S(2)}) collective-permute-start(bf16[4,18,1,128]{3,1,2,0:T(8,128)(2,1)S(1)} %get-tuple-element.476), channel_id=1, source_target_pairs={{1,0},{2,1},{3,2},{5,4},{6,5},{7,6},{9,8},{10,9},{11,10},{13,12},{... | collective-permute-start | bytes 55304 | tf_op jit(solution)/shard_map/while/body/eval_jaxpr/ppermute | solution.py:15
  150.3 6.5 %collective-permute-start.7 = (bf16[4,18,1,128]{3,1,2,0:T(8,128)(2,1)S(1)}, bf16[4,18,1,128]{3,1,2,0:T(8,128)(2,1)S(1)}, u32[]{:S(2)}, u32[]{:S(2)}) collective-permute-start(bf16[4,18,1,128]{3,1,2,0:T(8,128)(2,1)S(1)} %get-tuple-element.477), channel_id=1, source_target_pairs={{0,1},{1,2},{2,3},{4,5},{5,6},{6,7},{8,9},{9,10},{10,11},{12,13},{... | collective-permute-start | bytes 55304 | tf_op jit(solution)/shard_map/while/body/eval_jaxpr/ppermute | solution.py:12
  160.3 3.9 %collective-permute-start.8 = (bf16[4,16,32,128]{3,1,2,0:T(8,128)(2,1)S(1)}, bf16[4,16,32,128]{3,1,2,0:T(8,128)(2,1)}, u32[]{:S(2)}, u32[]{:S(2)}) collective-permute-start(bf16[4,16,32,128]{3,1,2,0:T(8,128)(2,1)S(1)} %slice_bitcast_fusion.7), channel_id=1, source_target_pairs={{16,0},{17,1},{18,2},{19,3},{20,4},{21,5},{22,6},{23,7},{24,8},{25... | collective-permute-start | bytes 1572872 | tf_op jit(solution)/shard_map/while/body/eval_jaxpr/ppermute | solution.py:23
  167.4 116.8 %copy-start.3 = (bf16[4,16,32,128]{3,2,1,0:T(8,128)(2,1)}, bf16[4,16,32,128]{3,2,1,0:T(8,128)(2,1)S(1)}, u32[]{:S(2)}) copy-start(bf16[4,16,32,128]{3,2,1,0:T(8,128)(2,1)S(1)} %scatter_fusion) | copy-start | bytes 1572868
  (12 other events, 22.7 us)
Sparse Core Ops, SparseCore 0:
  165.4 116.5 all-reduce.1
where the time goes:
time: 293 us; the launch traced here: 291 us
  waiting for transfers between devices  132 us (45%)
  starting transfers between devices  79.3 us (27%)
  matrix products  22.4 us (8%)
  local copies, waits for them, and re-layouts  21.9 us (7%)
  other arithmetic  20.5 us (7%)
  between operations  14.4 us (5%)
    psum x1, waiting for transfers between devices, local(): lax.psum(gathered.astype(jnp.bfloat16), ('row', 'col')).astype(jnp.float32)  115 us
    ppermute x12, starting transfers between devices, extended(): lax.ppermute(lax.slice_in_dim(block, block.shape[dim] - width, None, axis...  61.2 us
    ppermute x12, starting transfers between devices, extended(): lax.ppermute(lax.slice_in_dim(block, 0, width, axis=dim), axis, backward)  15.5 us
    dot_general x36, matrix products, kernel_terms(): lax.dot_general(window, flat_signal, (((0,), (0,)), ((), ())), preferred_...  12.2 us
    conv_general_dilated x6, matrix products, convolve(): lax.conv_general_dilated(padded, kernel, (1, 1), 'VALID', dimension_numbe...  10.2 us
    ppermute x12, waiting for transfers between devices, extended(): lax.ppermute(lax.slice_in_dim(block, block.shape[dim] - width, None, axis...  9.45 us
    ppermute x12, waiting for transfers between devices, extended(): lax.ppermute(lax.slice_in_dim(block, 0, width, axis=dim), axis, backward)  6.07 us
  transfers between devices with their start and end apart: 27, of which 15 were waited for; matrix products, arithmetic and copies ran while one was open for 6% of the time, Pallas kernels for 0%

commit v1 on v0

v1 whole, which is shorter than its diff:
```python
import jax
import jax.numpy as jnp
from jax import lax
from jax.sharding import PartitionSpec as P

AXES = ("section", "row", "col")


def sizes():
    return tuple(lax.axis_size(axis) for axis in AXES)


def flat_index(position, shape):
    section, row, col = position
    return (section * shape[1] + row) * shape[2] + col


def rim_piece(block, width, dr, dc):
    rows, cols = block.shape[1], block.shape[2]
    row_span = {-1: (rows - width, rows), 0: (0, rows), 1: (0, width)}[dr]
    col_span = {-1: (cols - width, cols), 0: (0, cols), 1: (0, width)}[dc]
    return block[:, row_span[0] : row_span[1], col_span[0] : col_span[1]]


def with_rim(block, width, from_section, sections_used):
    shape = sizes()
    bands = []
    for dr in (-1, 0, 1):
        band = []
        for dc in (-1, 0, 1):
            piece = rim_piece(block, width, dr, dc)
            if from_section == 0 and dr == 0 and dc == 0:
                band.append(piece)
                continue
            pairs = []
            for s in sections_used:
                for r in range(shape[1]):
                    for c in range(shape[2]):
                        source = (s + from_section, r + dr, c + dc)
                        if 0 <= source[0] < shape[0] and 0 <= source[1] < shape[1] and 0 <= source[2] < shape[2]:
                            pairs.append((flat_index(source, shape), flat_index((s, r, c), shape)))
            band.append(lax.ppermute(piece, AXES, pairs))
        bands.append(jnp.concatenate(band, axis=2))
    return jnp.concatenate(bands, axis=1)


def inside_mask(tile_rows, tile_cols, width):
    image_rows = tile_rows * lax.axis_size("row")
    image_cols = tile_cols * lax.axis_size("col")
    rows = lax.axis_index("row") * tile_rows - width + jnp.arange(tile_rows + 2 * width)
    cols = lax.axis_index("col") * tile_cols - width + jnp.arange(tile_cols + 2 * width)
    row_ok = (rows >= 0) & (rows < image_rows)
    col_ok = (cols >= 0) & (cols < image_cols)
    return (row_ok[:, None] & col_ok[None, :])[None, :, :, None]


def convolve(padded, kernel):
    return lax.conv_general_dilated(
        padded,
        kernel,
        (1, 1),
        "VALID",
        dimension_numbers=("NHWC", "HWIO", "NHWC"),
        preferred_element_type=jnp.float32,
    )


def kernel_terms(padded, signal):
    channels = signal.shape[3]
    flat_signal = signal.reshape(-1, channels)
    rows_out = []
    for a in range(3):
        tap_row = []
        for b in range(3):
            window = padded[:, a : a + signal.shape[1], b : b + signal.shape[2]].reshape(-1, channels)
            tap_row.append(
                lax.dot_general(
                    window,
                    flat_signal,
                    (((0,), (0,)), ((), ())),
                    preferred_element_type=jnp.float32,
                )
            )
        rows_out.append(jnp.stack(tap_row))
    return jnp.stack(rows_out)


def crop(block, width):
    return block[:, width : block.shape[1] - width, width : block.shape[2] - width]


def summed_over_tiles(grads, section):
    shape = sizes()
    steps = []
    for axis, dim in (("row", 1), ("col", 2)):
        distance = 1
        while distance < shape[dim]:
            steps.append((axis, dim, distance))
            distance *= 2

    def exchange(values, dim, distance):
        pairs = []
        sections_used = range(shape[0]) if section is None else (section,)
        for s in sections_used:
            for r in range(shape[1]):
                for c in range(shape[2]):
                    position = [s, r, c]
                    partner = list(position)
                    partner[dim] = position[dim] ^ distance
                    pairs.append((flat_index(position, shape), flat_index(partner, shape)))
        return lax.ppermute(values, AXES, pairs)

    current = grads.reshape(-1)
    kept = []
    for axis, dim, distance in steps:
        half = current.shape[0] // 2
        upper = (lax.axis_index(axis) // distance) % 2 == 1
        low, high = current[:half], current[half:]
        send = jnp.where(upper, low, high).astype(jnp.bfloat16)
        mine = jnp.where(upper, high, low).astype(jnp.bfloat16)
        other = exchange(send, dim, distance)
        current = mine.astype(jnp.float32) + other.astype(jnp.float32)
        kept.append((dim, distance, upper))
    current = current.astype(jnp.bfloat16)
    for dim, distance, upper in reversed(kept):
        other = exchange(current, dim, distance)
        current = jnp.where(
            upper, jnp.concatenate([other, current]), jnp.concatenate([current, other])
        )
    return current.astype(jnp.float32).reshape(grads.shape)


def local(checkpoints, kernels, cotangent, plan):
    sections_count, row_count, col_count = sizes()
    section_index = lax.axis_index("section")
    batches, tile_rows, tile_cols, channels = checkpoints.shape[1:]
    layer_count = kernels.shape[0]
    flipped = jnp.transpose(kernels[:, ::-1, ::-1], (0, 1, 2, 4, 3))
    inverse = jnp.sum(
        jnp.arange(batches)[:, None] * (plan[:, None] == jnp.arange(batches)[None, :]), axis=0
    )
    top_cotangent = jnp.take(cotangent, inverse, axis=0)

    rim = 2 * layer_count
    first = with_rim(checkpoints[0], rim, 0, range(sections_count))
    inputs_list = [first]
    current = first
    for layer_idx in range(layer_count):
        width = rim - layer_idx - 1
        current = jnp.tanh(convolve(current, kernels[layer_idx]))
        current = jnp.where(inside_mask(tile_rows, tile_cols, width), current, 0.0)
        current = current.astype(jnp.bfloat16)
        inputs_list.append(current)

    def backward(top_ext):
        gradient = top_ext.astype(jnp.float32)
        terms = [None] * layer_count
        for layer_idx in reversed(range(layer_count)):
            width = layer_idx
            output = crop(inputs_list[layer_idx + 1], 2 * (layer_count - layer_idx - 1))
            output = output.astype(jnp.float32)
            signal = gradient * (1.0 - output * output)
            signal = jnp.where(inside_mask(tile_rows, tile_cols, width + 1), signal, 0.0)
            signal = signal.astype(jnp.bfloat16)
            terms[layer_idx] = kernel_terms(
                crop(inputs_list[layer_idx], 2 * layer_count - layer_idx - 1),
                crop(signal, width + 1),
            )
            gradient = convolve(signal, flipped[layer_idx])
        return gradient.astype(jnp.bfloat16), jnp.stack(terms)

    top_ext = with_rim(top_cotangent, layer_count, 0, (sections_count - 1,))
    boundary = jnp.zeros((batches, tile_rows, tile_cols, channels), jnp.bfloat16)
    gathered = jnp.zeros((layer_count, 3, 3, channels, channels), jnp.float32)
    for tick in range(sections_count):
        active = sections_count - 1 - tick
        result, terms = backward(top_ext)
        is_active = section_index == active
        boundary = jnp.where(is_active, result, boundary)
        reduced = summed_over_tiles(terms, active)
        gathered = jnp.where(is_active, reduced, gathered)
        if tick + 1 < sections_count:
            top_ext = with_rim(result, layer_count, 1, (active - 1,))
    kernel_grad = gathered / batches
    return (boundary[None], kernel_grad)


def solution(mesh):
    return jax.shard_map(
        local,
        mesh=mesh,
        in_specs=(
            P("section", None, "row", "col", None),
            P("section", None, None, None, None),
            P(None, "row", "col", None),
            P(),
        ),
        out_specs=(P("section", None, "row", "col", None), P("section", None, None, None, None)),
        check_vma=False,
    )
```

time: 293 us -> 209 us (0.71)
  waiting for transfers between devices: 132 us -> 52.6 us
  between operations: 14.4 us -> 2.55 us
  local copies, waits for them, and re-layouts: 21.9 us -> 31.1 us
  matrix products: 22.4 us -> 28.6 us
  other arithmetic: 20.5 us -> 14.9 us
  starting transfers between devices: 79.3 us -> 76 us
    psum x1 -> x0, waiting for transfers between devices: 115 us -> none  [local(): lax.psum(gathered.astype(jnp.bfloat16), ('row', 'col')).astype(jnp.float32)]
    ppermute x26 -> x41, waiting for transfers between devices: 17.1 us -> 52.6 us  [the longest x25 33.4 us: with_rim(): band.append(lax.ppermute(piece, AXES, pairs))]
    unnamed x19 -> x42, local copies, waits for them, and re-layouts: 3.77 us -> 17.6 us
    while x26 -> x0, local copies, waits for them, and re-layouts: 6.18 us -> none
    slice x8, local copies, waits for them, and re-layouts: 1.12 us -> 6.91 us  [rim_piece(): return block[:, row_span[0]:row_span[1], col_span[0]:col_span[1]]]
    dot_general x36, matrix products: 12.2 us -> 17 us  [kernel_terms(): lax.dot_general(window, flat_signal, (((0,), (0,)), ((), ())), preferred_...]
    select_n x4 -> x8, other arithmetic: 3.71 us -> 0.39 us  [the longest x6 0.27 us: summed_over_tiles(): jnp.where(upper, jnp.concatenate([other, current]), jnp.concatenate([curr...]
    ppermute x26 -> x41, starting transfers between devices: 79.2 us -> 76 us  [the longest x25 39.2 us: with_rim(): band.append(lax.ppermute(piece, AXES, pairs))]
  transfers between devices with their start and end apart: 27 -> 41, of which waited for: 15 -> 11; matrix products, arithmetic and copies ran while one was open for 6% -> 19% of each run, Pallas kernels for 0% -> 0%
where the time goes in v1:
time: 209 us; the launch traced here: 206 us
  starting transfers between devices  76 us (36%)
  waiting for transfers between devices  52.6 us (25%)
  local copies, waits for them, and re-layouts  31.1 us (15%)
  matrix products  28.6 us (14%)
  other arithmetic  14.9 us (7%)
  between operations  2.55 us (1%)
    ppermute x25, starting transfers between devices, with_rim(): band.append(lax.ppermute(piece, AXES, pairs))  39.2 us
    ppermute x16, starting transfers between devices, exchange(): return lax.ppermute(values, AXES, pairs)  36.8 us
    ppermute x25, waiting for transfers between devices, with_rim(): band.append(lax.ppermute(piece, AXES, pairs))  33.4 us
    ppermute x16, waiting for transfers between devices, exchange(): return lax.ppermute(values, AXES, pairs)  19.2 us
    unnamed x42, local copies, waits for them, and re-layouts  17.6 us
    dot_general x36, matrix products, kernel_terms(): lax.dot_general(window, flat_signal, (((0,), (0,)), ((), ())), preferred_...  17 us
    conv_general_dilated x6, matrix products, convolve(): lax.conv_general_dilated(padded, kernel, (1, 1), 'VALID', dimension_numbe...  11.7 us
    slice x8, local copies, waits for them, and re-layouts, rim_piece(): return block[:, row_span[0]:row_span[1], col_span[0]:col_span[1]]  6.91 us
  transfers between devices with their start and end apart: 41, of which 11 were waited for; matrix products, arithmetic and copies ran while one was open for 19% of the time, Pallas kernels for 0%

profile of v1, /device:TPU:0, one launch (start us, length us, event | category | flops | bytes accessed | tf_op | source)
XLA Modules:
  0.0 205.8 jit_solution(1581977988461201902)
XLA Ops:
  2.1 5.9 %collective-permute-start.8 = (bf16[4,4,4,128]{3,2,1,0:T(4,128)(2,1)S(1)}, bf16[4,4,4,128]{3,2,1,0:T(4,128)(2,1)S(1)}, u32[]{:S(2)}, u32[]{:S(2)}) collective-permute-start(bf16[4,4,4,128]{3,2,1,0:T(4,128)(2,1)S(1)} %get-tuple-element.20), channel_id=1, source_target_pairs={{0,5},{1,6},{2,7},{4,9},{5,10},{6,11},{8,13},{9,14},{10,15},{16,21... | collective-permute-start | bytes 49160 | tf_op jit(solution)/shard_map/ppermute | solution.py:42
  11.4 1.7 fusion.121
  13.1 8.9 %collective-permute-start.11 = (bf16[4,16,4,128]{3,2,1,0:T(4,128)(2,1)}, bf16[4,16,4,128]{3,2,1,0:T(4,128)(2,1)S(1)}, u32[]{:S(2)}, u32[]{:S(2)}) collective-permute-start(bf16[4,16,4,128]{3,2,1,0:T(4,128)(2,1)} %get-tuple-element.26), channel_id=1, source_target_pairs={{0,1},{1,2},{2,3},{4,5},{5,6},{6,7},{8,9},{9,10},{10,11},{12,13},{... | collective-permute-start | bytes 196616 | tf_op jit(solution)/shard_map/ppermute | solution.py:42
  22.7 1.7 fusion.120
  29.8 4.7 %collective-permute-start.9 = (bf16[4,4,32,128]{3,2,1,0:T(8,128)(2,1)}, bf16[4,4,32,128]{3,2,1,0:T(8,128)(2,1)S(1)}, u32[]{:S(2)}, u32[]{:S(2)}) collective-permute-start(bf16[4,4,32,128]{3,2,1,0:T(8,128)(2,1)} %get-tuple-element.24), channel_id=1, source_target_pairs={{0,4},{1,5},{2,6},{3,7},{4,8},{5,9},{6,10},{7,11},{8,12},{9,13},{1... | collective-permute-start | bytes 393224 | tf_op jit(solution)/shard_map/ppermute | solution.py:42
  39.3 3.0 %collective-permute-done.14 = bf16[4,4,32,128]{3,2,1,0:T(8,128)(2,1)} collective-permute-done((bf16[4,4,32,128]{3,2,1,0:T(8,128)(2,1)}, bf16[4,4,32,128]{3,2,1,0:T(8,128)(2,1)}, u32[]{:S(2)}, u32[]{:S(2)}) %collective-permute-start.14) | collective-permute-done | bytes 131104 | tf_op jit(solution)/shard_map/ppermute | solution.py:42
  45.3 2.3 %select_tanh_fusion = bf16[22,32,5,128]{3,1,2,0:T(8,128)(2,1)S(1)} fusion(bf16[24,4,8,7,128]{4,0,3,2,1:T(8,128)(2,1)S(1)} %fusion.18, pred[32,5]{0,1:T(8,128)(4,1)S(1)} %copy-done.15, bf16[2,3,3,128,128]{4,3,2,1,0:T(8,128)(2,1)S(1)} %copy-done.2), kind=kOutput, calls=%fused_computation.13 | convolution fusion | flops 1038991360 | bytes 2573312 | tf_op jit(solution)/shard_map/conv_general_dilated | solution.py:58
  49.8 2.1 %select_tanh_fusion.1 = bf16[20,32,5,128]{3,1,2,0:T(8,128)(2,1)S(1)} fusion(bf16[22,4,8,7,128]{4,1,3,2,0:T(4,128)(2,1)S(1)} %fusion.23, pred[32,5]{0,1:T(8,128)(4,1)S(1)} %copy-done.14, bf16[2,3,3,128,128]{4,3,2,1,0:T(8,128)(2,1)S(1)} %copy-done.2), kind=kOutput, calls=%fused_computation.23 | convolution fusion | flops 944537600 | bytes 2376704 | tf_op jit(solution)/shard_map/conv_general_dilated | solution.py:58
  54.8 2.2 %fusion.9 = bf16[4,20,36,128]{3,2,1,0:T(8,128)(2,1)S(1)} fusion(bf16[4,2,2,128]{3,2,1,0:T(2,128)(2,1)S(1)} %collective-permute-done.7, bf16[4,2,32,128]{3,2,1,0:T(8,128)(2,1)S(1)} %collective-permute-done.6, bf16[4,2,2,128]{3,2,1,0:T(2,128)(2,1)S(1)} %collective-permute-done.5, bf16[4,16,2,128]{3,2,1,0:T(2,128)(2,1)S(1)} %collective-permute-done.4, ...), kind=kLoop, calls=%fused_computation.19 | loop fusion | flops 9216000 | bytes 2212560 | tf_op jit(solution)/shard_map/convert_element_type | solution.py:164
  62.1 1.9 convolution_select_fusion.3
  70.2 13.2 %copy.130 = bf16[18,4,34,128]{3,1,2,0:T(4,128)(2,1)S(1)} copy(bf16[18,4,34,128]{3,2,0,1:T(8,128)(2,1)S(1)} %bitcast.383) | data formatting | bytes 1253376
  86.9 1.7 fusion.21
  95.6 21.7 %collective-permute-done.24 = bf16[4,2,2,128]{3,2,1,0:T(2,128)(2,1)S(1)} collective-permute-done((bf16[4,2,2,128]{3,2,1,0:T(2,128)(2,1)S(1)}, bf16[4,2,2,128]{3,2,1,0:T(2,128)(2,1)S(1)}, u32[]{:S(2)}, u32[]{:S(2)}) %collective-permute-start.24) | collective-permute-done | bytes 4128 | tf_op jit(solution)/shard_map/ppermute | solution.py:42
  121.3 8.6 %collective-permute-done.21 = bf16[4,16,2,128]{3,2,1,0:T(2,128)(2,1)S(1)} collective-permute-done((bf16[4,16,2,128]{3,2,1,0:T(2,128)(2,1)S(1)}, bf16[4,16,2,128]{3,2,1,0:T(2,128)(2,1)S(1)}, u32[]{:S(2)}, u32[]{:S(2)}) %collective-permute-start.21) | collective-permute-done | bytes 32800 | tf_op jit(solution)/shard_map/ppermute | solution.py:42
  129.9 1.9 fusion.11
  136.8 1.9 convolution_select_fusion.2
  145.4 4.1 %collective-permute-start.25 = (bf16[147456]{0:T(1024)(128)(2,1)S(1)}, bf16[147456]{0:T(1024)(128)(2,1)S(1)}, u32[]{:S(2)}, u32[]{:S(2)}) collective-permute-start(bf16[147456]{0:T(1024)(128)(2,1)S(1)} %bitcast.396), channel_id=1, source_target_pairs={{0,4},{1,5},{2,6},{3,7},{4,0},{5,1},{6,2},{7,3},{8,12},{9,13},{10,... | collective-permute-start | bytes 884744 | tf_op jit(solution)/shard_map/ppermute | solution.py:111
  149.6 4.6 %collective-permute-done.25 = bf16[147456]{0:T(1024)(128)(2,1)S(1)} collective-permute-done((bf16[147456]{0:T(1024)(128)(2,1)S(1)}, bf16[147456]{0:T(1024)(128)(2,1)S(1)}, u32[]{:S(2)}, u32[]{:S(2)}) %collective-permute-start.25) | collective-permute-done | bytes 294944 | tf_op jit(solution)/shard_map/ppermute | solution.py:111
  154.3 4.5 %collective-permute-start.26 = (bf16[73728]{0:T(1024)(128)(2,1)S(1)}, bf16[73728]{0:T(1024)(128)(2,1)S(1)}, u32[]{:S(2)}, u32[]{:S(2)}) collective-permute-start(bf16[73728]{0:T(1024)(128)(2,1)S(1)} %select_convert_fusion.6), channel_id=1, source_target_pairs={{0,8},{1,9},{2,10},{3,11},{4,12},{5,13},{6,14},{7,15},{8,0},{9,1},... | collective-permute-start | bytes 442376 | tf_op jit(solution)/shard_map/ppermute | solution.py:111
  160.1 1.8 collective-permute-done.26
  162.0 4.3 %collective-permute-start.27 = (bf16[36864]{0:T(1024)(128)(2,1)S(1)}, bf16[36864]{0:T(1024)(128)(2,1)S(1)}, u32[]{:S(2)}, u32[]{:S(2)}) collective-permute-start(bf16[36864]{0:T(1024)(128)(2,1)S(1)} %select_convert_fusion.10), channel_id=1, source_target_pairs={{0,1},{1,0},{2,3},{3,2},{4,5},{5,4},{6,7},{7,6},{8,9},{9,8},{10,11... | collective-permute-start | bytes 221192 | tf_op jit(solution)/shard_map/ppermute | solution.py:111
  166.7 1.9 collective-permute-done.27
  168.6 3.7 %collective-permute-start.28 = (bf16[18432]{0:T(1024)(128)(2,1)S(1)}, bf16[18432]{0:T(1024)(128)(2,1)S(1)}, u32[]{:S(2)}, u32[]{:S(2)}) collective-permute-start(bf16[18432]{0:T(1024)(128)(2,1)S(1)} %select_convert_fusion.14), channel_id=1, source_target_pairs={{0,2},{1,3},{2,0},{3,1},{4,6},{5,7},{6,4},{7,5},{8,10},{9,11},{10,... | collective-permute-start | bytes 110600 | tf_op jit(solution)/shard_map/ppermute | solution.py:111
  173.1 2.3 %collective-permute-done.28 = bf16[18432]{0:T(1024)(128)(2,1)S(1)} collective-permute-done((bf16[18432]{0:T(1024)(128)(2,1)S(1)}, bf16[18432]{0:T(1024)(128)(2,1)S(1)}, u32[]{:S(2)}, u32[]{:S(2)}) %collective-permute-start.28) | collective-permute-done | bytes 36896 | tf_op jit(solution)/shard_map/ppermute | solution.py:111
  175.4 3.7 %collective-permute-start.29 = (bf16[18432]{0:T(1024)(128)(2,1)S(1)}, bf16[18432]{0:T(1024)(128)(2,1)S(1)}, u32[]{:S(2)}, u32[]{:S(2)}) collective-permute-start(bf16[18432]{0:T(1024)(128)(2,1)S(1)} %add_convert_fusion.1), channel_id=1, source_target_pairs={{0,2},{1,3},{2,0},{3,1},{4,6},{5,7},{6,4},{7,5},{8,10},{9,11},{10,... | collective-permute-start | bytes 110600 | tf_op jit(solution)/shard_map/ppermute | solution.py:111
  179.8 2.3 %collective-permute-done.29 = bf16[18432]{0:T(1024)(128)(2,1)S(1)} collective-permute-done((bf16[18432]{0:T(1024)(128)(2,1)S(1)}, bf16[18432]{0:T(1024)(128)(2,1)S(1)}, u32[]{:S(2)}, u32[]{:S(2)}) %collective-permute-start.29) | collective-permute-done | bytes 36896 | tf_op jit(solution)/shard_map/ppermute | solution.py:111
  182.2 3.9 %collective-permute-start.30 = (bf16[36864]{0:T(1024)(128)(2,1)S(1)}, bf16[36864]{0:T(1024)(128)(2,1)S(1)}, u32[]{:S(2)}, u32[]{:S(2)}) collective-permute-start(bf16[36864]{0:T(1024)(128)(2,1)S(1)} %maximum_select_fusion.6), channel_id=1, source_target_pairs={{0,1},{1,0},{2,3},{3,2},{4,5},{5,4},{6,7},{7,6},{8,9},{9,8},{10,11... | collective-permute-start | bytes 221192 | tf_op jit(solution)/shard_map/ppermute | solution.py:111
  188.5 3.9 %collective-permute-start.31 = (bf16[73728]{0:T(1024)(128)(2,1)S(1)}, bf16[73728]{0:T(1024)(128)(2,1)S(1)}, u32[]{:S(2)}, u32[]{:S(2)}) collective-permute-start(bf16[73728]{0:T(1024)(128)(2,1)S(1)} %maximum_select_fusion.4), channel_id=1, source_target_pairs={{0,8},{1,9},{2,10},{3,11},{4,12},{5,13},{6,14},{7,15},{8,0},{9,1},... | collective-permute-start | bytes 442376 | tf_op jit(solution)/shard_map/ppermute | solution.py:111
  193.2 2.3 %collective-permute-done.31 = bf16[73728]{0:T(1024)(128)(2,1)S(1)} collective-permute-done((bf16[73728]{0:T(1024)(128)(2,1)S(1)}, bf16[73728]{0:T(1024)(128)(2,1)S(1)}, u32[]{:S(2)}, u32[]{:S(2)}) %collective-permute-start.31) | collective-permute-done | bytes 147488 | tf_op jit(solution)/shard_map/ppermute | solution.py:111
  195.6 3.3 %collective-permute-start.32 = (bf16[147456]{0:T(1024)(128)(2,1)S(1)}, bf16[147456]{0:T(1024)(128)(2,1)S(1)}, u32[]{:S(2)}, u32[]{:S(2)}) collective-permute-start(bf16[147456]{0:T(1024)(128)(2,1)S(1)} %maximum_select_fusion.2), channel_id=1, source_target_pairs={{0,4},{1,5},{2,6},{3,7},{4,0},{5,1},{6,2},{7,3},{8,12},{9,13},{10,... | collective-permute-start | bytes 884744 | tf_op jit(solution)/shard_map/ppermute | solution.py:111
  198.9 1.7 fusion.26
  201.9 2.3 %collective-permute-done.32 = bf16[147456]{0:T(1024)(128)(2,1)S(1)} collective-permute-done((bf16[147456]{0:T(1024)(128)(2,1)S(1)}, bf16[147456]{0:T(1024)(128)(2,1)S(1)}, u32[]{:S(2)}, u32[]{:S(2)}) %collective-permute-start.32) | collective-permute-done | bytes 294944 | tf_op jit(solution)/shard_map/ppermute | solution.py:111
  (230 shorter events, 69.1 us)
Async XLA Ops:
  2.1 25.7 %collective-permute-start.8 = (bf16[4,4,4,128]{3,2,1,0:T(4,128)(2,1)S(1)}, bf16[4,4,4,128]{3,2,1,0:T(4,128)(2,1)S(1)}, u32[]{:S(2)}, u32[]{:S(2)}) collective-permute-start(bf16[4,4,4,128]{3,2,1,0:T(4,128)(2,1)S(1)} %get-tuple-element.20), channel_id=1, source_target_pairs={{0,5},{1,6},{2,7},{4,9},{5,10},{6,11},{8,13},{9,14},{10,15},{16,21... | collective-permute-start | bytes 49160 | tf_op jit(solution)/shard_map/ppermute | solution.py:42
  8.0 21.1 %collective-permute-start.15 = (bf16[4,4,4,128]{3,2,1,0:T(4,128)(2,1)S(1)}, bf16[4,4,4,128]{3,2,1,0:T(4,128)(2,1)S(1)}, u32[]{:S(2)}, u32[]{:S(2)}) collective-permute-start(bf16[4,4,4,128]{3,2,1,0:T(4,128)(2,1)S(1)} %get-tuple-element.21), channel_id=1, source_target_pairs={{5,0},{6,1},{7,2},{9,4},{10,5},{11,6},{13,8},{14,9},{15,10},{21,16... | collective-permute-start | bytes 49160 | tf_op jit(solution)/shard_map/ppermute | solution.py:42
  9.3 25.2 %collective-permute-start.13 = (bf16[4,4,4,128]{3,2,1,0:T(4,128)(2,1)S(1)}, bf16[4,4,4,128]{3,2,1,0:T(4,128)(2,1)S(1)}, u32[]{:S(2)}, u32[]{:S(2)}) collective-permute-start(bf16[4,4,4,128]{3,2,1,0:T(4,128)(2,1)S(1)} %get-tuple-element.22), channel_id=1, source_target_pairs={{4,1},{5,2},{6,3},{8,5},{9,6},{10,7},{12,9},{13,10},{14,11},{20,17... | collective-permute-start | bytes 49160 | tf_op jit(solution)/shard_map/ppermute | solution.py:42
  10.0 26.5 %collective-permute-start.10 = (bf16[4,4,4,128]{3,2,1,0:T(4,128)(2,1)}, bf16[4,4,4,128]{3,2,1,0:T(4,128)(2,1)}, u32[]{:S(2)}, u32[]{:S(2)}) collective-permute-start(bf16[4,4,4,128]{3,2,1,0:T(4,128)(2,1)} %get-tuple-element.23), channel_id=1, source_target_pairs={{1,4},{2,5},{3,6},{5,8},{6,9},{7,10},{9,12},{10,13},{11,14},{17,20... | collective-permute-start | bytes 49160 | tf_op jit(solution)/shard_map/ppermute | solution.py:42
  13.1 24.1 %collective-permute-start.11 = (bf16[4,16,4,128]{3,2,1,0:T(4,128)(2,1)}, bf16[4,16,4,128]{3,2,1,0:T(4,128)(2,1)S(1)}, u32[]{:S(2)}, u32[]{:S(2)}) collective-permute-start(bf16[4,16,4,128]{3,2,1,0:T(4,128)(2,1)} %get-tuple-element.26), channel_id=1, source_target_pairs={{0,1},{1,2},{2,3},{4,5},{5,6},{6,7},{8,9},{9,10},{10,11},{12,13},{... | collective-permute-start | bytes 196616 | tf_op jit(solution)/shard_map/ppermute | solution.py:42
  27.9 10.1 %collective-permute-start.12 = (bf16[4,16,4,128]{3,2,1,0:T(4,128)(2,1)}, bf16[4,16,4,128]{3,2,1,0:T(4,128)(2,1)}, u32[]{:S(2)}, u32[]{:S(2)}) collective-permute-start(bf16[4,16,4,128]{3,2,1,0:T(4,128)(2,1)} %get-tuple-element.27), channel_id=1, source_target_pairs={{1,0},{2,1},{3,2},{5,4},{6,5},{7,6},{9,8},{10,9},{11,10},{13,12},{... | collective-permute-start | bytes 196616 | tf_op jit(solution)/shard_map/ppermute | solution.py:42
  29.8 8.8 %collective-permute-start.9 = (bf16[4,4,32,128]{3,2,1,0:T(8,128)(2,1)}, bf16[4,4,32,128]{3,2,1,0:T(8,128)(2,1)S(1)}, u32[]{:S(2)}, u32[]{:S(2)}) collective-permute-start(bf16[4,4,32,128]{3,2,1,0:T(8,128)(2,1)} %get-tuple-element.24), channel_id=1, source_target_pairs={{0,4},{1,5},{2,6},{3,7},{4,8},{5,9},{6,10},{7,11},{8,12},{9,13},{1... | collective-permute-start | bytes 393224 | tf_op jit(solution)/shard_map/ppermute | solution.py:42
  35.1 7.2 %collective-permute-start.14 = (bf16[4,4,32,128]{3,2,1,0:T(8,128)(2,1)}, bf16[4,4,32,128]{3,2,1,0:T(8,128)(2,1)}, u32[]{:S(2)}, u32[]{:S(2)}) collective-permute-start(bf16[4,4,32,128]{3,2,1,0:T(8,128)(2,1)} %get-tuple-element.25), channel_id=1, source_target_pairs={{4,0},{5,1},{6,2},{7,3},{8,4},{9,5},{10,6},{11,7},{12,8},{13,9},{1... | collective-permute-start | bytes 393224 | tf_op jit(solution)/shard_map/ppermute | solution.py:42
  36.6 15.3 %collective-permute-start = (bf16[4,2,2,128]{3,2,1,0:T(2,128)(2,1)}, bf16[4,2,2,128]{3,2,1,0:T(2,128)(2,1)S(1)}, u32[]{:S(2)}, u32[]{:S(2)}) collective-permute-start(bf16[4,2,2,128]{3,2,1,0:T(2,128)(2,1)} %get-tuple-element.28), channel_id=1, source_target_pairs={{16,21},{17,22},{18,23},{20,25},{21,26},{22,27},{24,29},{25,30},{2... | collective-permute-start | bytes 12296 | tf_op jit(solution)/shard_map/ppermute | solution.py:42
  37.2 15.3 %collective-permute-start.7 = (bf16[4,2,2,128]{3,2,1,0:T(2,128)(2,1)}, bf16[4,2,2,128]{3,2,1,0:T(2,128)(2,1)S(1)}, u32[]{:S(2)}, u32[]{:S(2)}) collective-permute-start(bf16[4,2,2,128]{3,2,1,0:T(2,128)(2,1)} %get-tuple-element.29), channel_id=1, source_target_pairs={{21,16},{22,17},{23,18},{25,20},{26,21},{27,22},{29,24},{30,25},{3... | collective-permute-start | bytes 12296 | tf_op jit(solution)/shard_map/ppermute | solution.py:42
  37.9 15.3 %collective-permute-start.5 = (bf16[4,2,2,128]{3,2,1,0:T(2,128)(2,1)}, bf16[4,2,2,128]{3,2,1,0:T(2,128)(2,1)S(1)}, u32[]{:S(2)}, u32[]{:S(2)}) collective-permute-start(bf16[4,2,2,128]{3,2,1,0:T(2,128)(2,1)} %get-tuple-element.30), channel_id=1, source_target_pairs={{20,17},{21,18},{22,19},{24,21},{25,22},{26,23},{28,25},{29,26},{3... | collective-permute-start | bytes 12296 | tf_op jit(solution)/shard_map/ppermute | solution.py:42
  38.6 16.1 %collective-permute-start.2 = (bf16[4,2,2,128]{3,2,1,0:T(2,128)(2,1)S(1)}, bf16[4,2,2,128]{3,2,1,0:T(2,128)(2,1)S(1)}, u32[]{:S(2)}, u32[]{:S(2)}) collective-permute-start(bf16[4,2,2,128]{3,2,1,0:T(2,128)(2,1)S(1)} %get-tuple-element.31), channel_id=1, source_target_pairs={{17,20},{18,21},{19,22},{21,24},{22,25},{23,26},{25,28},{26,29},{2... | collective-permute-start | bytes 12296 | tf_op jit(solution)/shard_map/ppermute | solution.py:42
  42.3 12.4 %collective-permute-start.3 = (bf16[4,16,2,128]{3,2,1,0:T(2,128)(2,1)}, bf16[4,16,2,128]{3,2,1,0:T(2,128)(2,1)S(1)}, u32[]{:S(2)}, u32[]{:S(2)}) collective-permute-start(bf16[4,16,2,128]{3,2,1,0:T(2,128)(2,1)} %get-tuple-element.34), channel_id=1, source_target_pairs={{16,17},{17,18},{18,19},{20,21},{21,22},{22,23},{24,25},{25,26},{2... | collective-permute-start | bytes 98312 | tf_op jit(solution)/shard_map/ppermute | solution.py:42
  86.2 7.1 %collective-permute-start.33 = (bf16[147456]{0:T(1024)(128)(2,1)S(1)}, bf16[147456]{0:T(1024)(128)(2,1)S(1)}, u32[]{:S(2)}, u32[]{:S(2)}) collective-permute-start(bf16[147456]{0:T(1024)(128)(2,1)S(1)} %bitcast.395), channel_id=1, source_target_pairs={{16,20},{17,21},{18,22},{19,23},{20,16},{21,17},{22,18},{23,19},{2... | collective-permute-start | bytes 884744 | tf_op jit(solution)/shard_map/ppermute | solution.py:111
  89.3 40.5 %collective-permute-start.20 = (bf16[4,16,32,128]{3,2,1,0:T(8,128)(2,1)S(1)}, bf16[4,16,32,128]{3,2,1,0:T(8,128)(2,1)S(1)}, u32[]{:S(2)}, u32[]{:S(2)}) collective-permute-start(bf16[4,16,32,128]{3,2,1,0:T(8,128)(2,1)S(1)} %bitcast.390), channel_id=1, source_target_pairs={{16,0},{17,1},{18,2},{19,3},{20,4},{21,5},{22,6},{23,7},{24,8},{25... | collective-permute-start | bytes 1572872 | tf_op jit(solution)/shard_map/ppermute | solution.py:42
  91.3 25.9 %collective-permute-start.24 = (bf16[4,2,2,128]{3,2,1,0:T(2,128)(2,1)S(1)}, bf16[4,2,2,128]{3,2,1,0:T(2,128)(2,1)S(1)}, u32[]{:S(2)}, u32[]{:S(2)}) collective-permute-start(bf16[4,2,2,128]{3,2,1,0:T(2,128)(2,1)S(1)} %get-tuple-element.15), channel_id=1, source_target_pairs={{21,0},{22,1},{23,2},{25,4},{26,5},{27,6},{29,8},{30,9},{31,10}} | collective-permute-start | bytes 12296 | tf_op jit(solution)/shard_map/ppermute | solution.py:42
  92.6 25.9 %collective-permute-start.22 = (bf16[4,2,2,128]{3,2,1,0:T(2,128)(2,1)S(1)}, bf16[4,2,2,128]{3,2,1,0:T(2,128)(2,1)S(1)}, u32[]{:S(2)}, u32[]{:S(2)}) collective-permute-start(bf16[4,2,2,128]{3,2,1,0:T(2,128)(2,1)S(1)} %get-tuple-element.16), channel_id=1, source_target_pairs={{20,1},{21,2},{22,3},{24,5},{25,6},{26,7},{28,9},{29,10},{30,11}} | collective-permute-start | bytes 12296 | tf_op jit(solution)/shard_map/ppermute | solution.py:42
  94.2 25.1 %collective-permute-start.18 = (bf16[4,2,2,128]{3,2,1,0:T(2,128)(2,1)S(1)}, bf16[4,2,2,128]{3,2,1,0:T(2,128)(2,1)S(1)}, u32[]{:S(2)}, u32[]{:S(2)}) collective-permute-start(bf16[4,2,2,128]{3,2,1,0:T(2,128)(2,1)S(1)} %get-tuple-element.17), channel_id=1, source_target_pairs={{17,4},{18,5},{19,6},{21,8},{22,9},{23,10},{25,12},{26,13},{27,14}} | collective-permute-start | bytes 12296 | tf_op jit(solution)/shard_map/ppermute | solution.py:42
  94.9 35.0 %collective-permute-start.17 = (bf16[4,2,32,128]{3,2,1,0:T(8,128)(2,1)S(1)}, bf16[4,2,32,128]{3,2,1,0:T(8,128)(2,1)S(1)}, u32[]{:S(2)}, u32[]{:S(2)}) collective-permute-start(bf16[4,2,32,128]{3,2,1,0:T(8,128)(2,1)S(1)} %bitcast.399), channel_id=1, source_target_pairs={{16,4},{17,5},{18,6},{19,7},{20,8},{21,9},{22,10},{23,11},{24,12},... | collective-permute-start | bytes 196616 | tf_op jit(solution)/shard_map/ppermute | solution.py:42
  117.3 12.6 %collective-permute-start.23 = (bf16[4,2,32,128]{3,2,1,0:T(8,128)(2,1)S(1)}, bf16[4,2,32,128]{3,2,1,0:T(8,128)(2,1)S(1)}, u32[]{:S(2)}, u32[]{:S(2)}) collective-permute-start(bf16[4,2,32,128]{3,2,1,0:T(8,128)(2,1)S(1)} %bitcast.400), channel_id=1, source_target_pairs={{20,0},{21,1},{22,2},{23,3},{24,4},{25,5},{26,6},{27,7},{28,8},{29... | collective-permute-start | bytes 196616 | tf_op jit(solution)/shard_map/ppermute | solution.py:42
  119.3 10.6 %collective-permute-start.21 = (bf16[4,16,2,128]{3,2,1,0:T(2,128)(2,1)S(1)}, bf16[4,16,2,128]{3,2,1,0:T(2,128)(2,1)S(1)}, u32[]{:S(2)}, u32[]{:S(2)}) collective-permute-start(bf16[4,16,2,128]{3,2,1,0:T(2,128)(2,1)S(1)} %get-tuple-element.19), channel_id=1, source_target_pairs={{17,0},{18,1},{19,2},{21,4},{22,5},{23,6},{25,8},{26,9},{27,10},{2... | collective-permute-start | bytes 98312 | tf_op jit(solution)/shard_map/ppermute | solution.py:42
  120.6 28.9 %collective-permute-start.35 = (bf16[36864]{0:T(1024)(128)(2,1)S(1)}, bf16[36864]{0:T(1024)(128)(2,1)S(1)}, u32[]{:S(2)}, u32[]{:S(2)}) collective-permute-start(bf16[36864]{0:T(1024)(128)(2,1)S(1)} %select_convert_fusion.8), channel_id=1, source_target_pairs={{16,17},{17,16},{18,19},{19,18},{20,21},{21,20},{22,23},{23,22},{2... | collective-permute-start | bytes 221192 | tf_op jit(solution)/shard_map/ppermute | solution.py:111
  145.4 8.8 %collective-permute-start.25 = (bf16[147456]{0:T(1024)(128)(2,1)S(1)}, bf16[147456]{0:T(1024)(128)(2,1)S(1)}, u32[]{:S(2)}, u32[]{:S(2)}) collective-permute-start(bf16[147456]{0:T(1024)(128)(2,1)S(1)} %bitcast.396), channel_id=1, source_target_pairs={{0,4},{1,5},{2,6},{3,7},{4,0},{5,1},{6,2},{7,3},{8,12},{9,13},{10,... | collective-permute-start | bytes 884744 | tf_op jit(solution)/shard_map/ppermute | solution.py:111
  154.3 7.6 %collective-permute-start.26 = (bf16[73728]{0:T(1024)(128)(2,1)S(1)}, bf16[73728]{0:T(1024)(128)(2,1)S(1)}, u32[]{:S(2)}, u32[]{:S(2)}) collective-permute-start(bf16[73728]{0:T(1024)(128)(2,1)S(1)} %select_convert_fusion.6), channel_id=1, source_target_pairs={{0,8},{1,9},{2,10},{3,11},{4,12},{5,13},{6,14},{7,15},{8,0},{9,1},... | collective-permute-start | bytes 442376 | tf_op jit(solution)/shard_map/ppermute | solution.py:111
  158.8 13.6 %collective-permute-start.36 = (bf16[18432]{0:T(1024)(128)(2,1)S(1)}, bf16[18432]{0:T(1024)(128)(2,1)S(1)}, u32[]{:S(2)}, u32[]{:S(2)}) collective-permute-start(bf16[18432]{0:T(1024)(128)(2,1)S(1)} %select_convert_fusion.12), channel_id=1, source_target_pairs={{16,18},{17,19},{18,16},{19,17},{20,22},{21,23},{22,20},{23,21},{2... | collective-permute-start | bytes 110600 | tf_op jit(solution)/shard_map/ppermute | solution.py:111
  168.6 6.8 %collective-permute-start.28 = (bf16[18432]{0:T(1024)(128)(2,1)S(1)}, bf16[18432]{0:T(1024)(128)(2,1)S(1)}, u32[]{:S(2)}, u32[]{:S(2)}) collective-permute-start(bf16[18432]{0:T(1024)(128)(2,1)S(1)} %select_convert_fusion.14), channel_id=1, source_target_pairs={{0,2},{1,3},{2,0},{3,1},{4,6},{5,7},{6,4},{7,5},{8,10},{9,11},{10,... | collective-permute-start | bytes 110600 | tf_op jit(solution)/shard_map/ppermute | solution.py:111
  172.4 6.7 %collective-permute-start.37 = (bf16[18432]{0:T(1024)(128)(2,1)S(1)}, bf16[18432]{0:T(1024)(128)(2,1)S(1)}, u32[]{:S(2)}, u32[]{:S(2)}) collective-permute-start(bf16[18432]{0:T(1024)(128)(2,1)S(1)} %add_convert_fusion), channel_id=1, source_target_pairs={{16,18},{17,19},{18,16},{19,17},{20,22},{21,23},{22,20},{23,21},{2... | collective-permute-start | bytes 110600 | tf_op jit(solution)/shard_map/ppermute | solution.py:111
  175.4 6.8 %collective-permute-start.29 = (bf16[18432]{0:T(1024)(128)(2,1)S(1)}, bf16[18432]{0:T(1024)(128)(2,1)S(1)}, u32[]{:S(2)}, u32[]{:S(2)}) collective-permute-start(bf16[18432]{0:T(1024)(128)(2,1)S(1)} %add_convert_fusion.1), channel_id=1, source_target_pairs={{0,2},{1,3},{2,0},{3,1},{4,6},{5,7},{6,4},{7,5},{8,10},{9,11},{10,... | collective-permute-start | bytes 110600 | tf_op jit(solution)/shard_map/ppermute | solution.py:111
  179.2 6.9 %collective-permute-start.38 = (bf16[36864]{0:T(1024)(128)(2,1)S(1)}, bf16[36864]{0:T(1024)(128)(2,1)S(1)}, u32[]{:S(2)}, u32[]{:S(2)}) collective-permute-start(bf16[36864]{0:T(1024)(128)(2,1)S(1)} %maximum_select_fusion.7), channel_id=1, source_target_pairs={{16,17},{17,16},{18,19},{19,18},{20,21},{21,20},{22,23},{23,22},{2... | collective-permute-start | bytes 221192 | tf_op jit(solution)/shard_map/ppermute | solution.py:111
  188.5 7.0 %collective-permute-start.31 = (bf16[73728]{0:T(1024)(128)(2,1)S(1)}, bf16[73728]{0:T(1024)(128)(2,1)S(1)}, u32[]{:S(2)}, u32[]{:S(2)}) collective-permute-start(bf16[73728]{0:T(1024)(128)(2,1)S(1)} %maximum_select_fusion.4), channel_id=1, source_target_pairs={{0,8},{1,9},{2,10},{3,11},{4,12},{5,13},{6,14},{7,15},{8,0},{9,1},... | collective-permute-start | bytes 442376 | tf_op jit(solution)/shard_map/ppermute | solution.py:111
  192.5 9.4 %collective-permute-start.40 = (bf16[147456]{0:T(1024)(128)(2,1)S(1)}, bf16[147456]{0:T(1024)(128)(2,1)S(1)}, u32[]{:S(2)}, u32[]{:S(2)}) collective-permute-start(bf16[147456]{0:T(1024)(128)(2,1)S(1)} %maximum_select_fusion.3), channel_id=1, source_target_pairs={{16,20},{17,21},{18,22},{19,23},{20,16},{21,17},{22,18},{23,19},{2... | collective-permute-start | bytes 884744 | tf_op jit(solution)/shard_map/ppermute | solution.py:111
  195.6 8.6 %collective-permute-start.32 = (bf16[147456]{0:T(1024)(128)(2,1)S(1)}, bf16[147456]{0:T(1024)(128)(2,1)S(1)}, u32[]{:S(2)}, u32[]{:S(2)}) collective-permute-start(bf16[147456]{0:T(1024)(128)(2,1)S(1)} %maximum_select_fusion.2), channel_id=1, source_target_pairs={{0,4},{1,5},{2,6},{3,7},{4,0},{5,1},{6,2},{7,3},{8,12},{9,13},{10,... | collective-permute-start | bytes 884744 | tf_op jit(solution)/shard_map/ppermute | solution.py:111
  (25 other events, 109.9 us)
